TPU v7x, 32 devices: a whole 2x2x4 slice. The times are simulated.
32 devices in a mesh: seq: 4 (over y, core), batch: 8 (over z, x).
Axes of the slice: x: 2, y: 2, z: 4, core: 2. Of those that a mesh axis runs over, the one named last changes fastest.
Arguments:
- inputs: bfloat16 [8, 512, 768], P('batch', 'seq'), may hold values from -6 to 6
- cotangent: bfloat16 [8, 512, 768], P('batch', 'seq'), may hold values from -6 to 6
- weight: bfloat16 [768, 2304], replicated, may hold values from -0.125 to 0.125
Outputs:
- grad_input: bfloat16 [8, 512, 768], P('batch', 'seq')
- grad_weight: float32 [768, 2304], P('seq', 'batch')
All inputs are finite; a program needn't handle non-finite values.
Results may differ from a plain program's by a relative error of at most 0.0026.
Values may be sent and summed in bfloat16 or wider, within the bound.
No kernel may reach another device: no remote copies, remote signals or barrier semaphores. Data moves between devices by JAX's collectives and lax.ppermute only.
A program may use at most 64 MiB of HBM per device.

v0:
```python
import math
import jax
import jax.numpy as jnp
from jax import lax
from jax.sharding import PartitionSpec as P

KW = 3
TAP_SPACING = 64


def extended_2(x, sides, width):
    for axis, dim in sides:
        peers, length = (lax.axis_size(axis), x.shape[dim])
        up = [(i, (i + 1) % peers) for i in range(peers - 1)]
        down = [(j, i) for i, j in up]
        last = lax.slice_in_dim(x, length - width, length, axis=dim)
        first = lax.slice_in_dim(x, 0, width, axis=dim)
        before = lax.ppermute(last, axis, up)
        after = lax.ppermute(first, axis, down)
        x = jnp.concatenate([before, x, after], axis=dim)
    return x


def gelu_factors(values):
    normal_cdf = 0.5 * (1.0 + jax.scipy.special.erf(values / math.sqrt(2.0)))
    density = jnp.exp(-0.5 * values * values) / math.sqrt(2.0 * math.pi)
    return (values * normal_cdf, normal_cdf + values * density)


def body(inputs, cotangent, weight):
    middle_offset = KW // 2
    reach = middle_offset * TAP_SPACING
    length = inputs.shape[1]
    in_width = inputs.shape[2]
    padded_input = extended_2(cotangent, (("seq", 1),), reach)
    extended = padded_input[0]
    values = inputs[0].astype(jnp.float32)
    activation, deriv = gelu_factors(values)
    act = activation.astype(jnp.bfloat16)
    grad_act = jnp.zeros((length, in_width), jnp.float32)
    for tap_index in range(KW):
        window_start = (2 * middle_offset - tap_index) * TAP_SPACING
        window = lax.slice_in_dim(extended, window_start, window_start + length, axis=0)
        grad_act = grad_act + jnp.dot(
            window,
            weight[:, tap_index * in_width : (tap_index + 1) * in_width],
            preferred_element_type=jnp.float32,
        )
    grad_input = (grad_act * deriv).astype(jnp.bfloat16)[None]
    seq_count = lax.axis_size("seq")
    batch_count = lax.axis_size("batch")
    counted = batch_count * inputs.shape[0] * length * seq_count
    factor = 1.0 / math.sqrt(float(counted))
    owned = lax.all_to_all(cotangent, "seq", split_axis=2, concat_axis=1, tiled=True)[0]
    own_rows = owned.shape[1]
    owned_padded = jnp.pad(owned, ((reach, reach), (0, 0)))
    whole_act = lax.all_gather(act[None], "seq", axis=1, tiled=True)[0]
    count = whole_act.shape[0]
    updated = []
    for tap_index in range(KW):
        offset = 0 + (2 * middle_offset - tap_index) * TAP_SPACING
        window = lax.dynamic_slice_in_dim(owned_padded, offset, count, 0)
        updated.append(
            lax.dot_general(
                window, whole_act, (((0,), (0,)), ((), ())), preferred_element_type=jnp.float32
            )
        )
    taps_sum = jnp.stack(updated, axis=0)
    local_rows = jnp.transpose(taps_sum, (1, 0, 2)).reshape(own_rows, KW * in_width) * factor
    pieces = local_rows.reshape(own_rows, batch_count, -1)
    swapped = lax.all_to_all(pieces, "batch", split_axis=1, concat_axis=1, tiled=True)
    grad_weight = jnp.sum(swapped, axis=1)
    return (grad_input, grad_weight)


def solution(mesh):
    placed = (P("batch", "seq", None), P("batch", "seq", None), P())
    return jax.shard_map(
        body,
        mesh=mesh,
        in_specs=placed,
        out_specs=(P("batch", "seq", None), P("seq", "batch")),
        check_vma=False,
    )
```

profile of v0, /device:TPU:0, one launch (start us, length us, event | category | flops | bytes accessed | tf_op | source)
XLA Modules:
  0.0 85.2 jit_solution(1251447381360411007)
XLA Ops:
  0.6 0.0 copy-start.1
  0.6 1.3 %copy.8 = bf16[1,128,768]{1,0,2:T(2,128)(2,1)S(1)} copy(bf16[1,128,768]{2,1,0:T(8,128)(2,1)} %param.4) | data formatting | bytes 393216 | tf_op args[1]
  2.0 0.5 broadcast.12
  2.5 1.8 %reduce = bf16[768,128]{1,0:T(8,128)(2,1)S(1)} reduce(bf16[768,1,128]{2,1,0:T(2,128)(2,1)S(1)} %bitcast.78, bf16[]{:T(256)} %broadcast.12), dimensions={1}, to_apply=%bitcast.69.reduce_sub_computation | reduce | bytes 393218
  4.3 0.7 reshape.16
  5.0 4.2 %all-to-all-start = ((bf16[4,2,12288]{2,1,0:T(2,128)(2,1)}), bf16[4,2,12288]{2,1,0:T(2,128)(2,1)S(1)}, u32[]{:S(2)}, u32[]{:S(2)}) async-start(bf16[4,2,12288]{2,1,0:T(2,128)(2,1)} %reshape.16), calls=%async_computation | async-start | bytes 393216 | tf_op jit(solution)/shard_map/all_to_all | solution.py:54
  9.2 0.0 copy-done.1
  9.2 0.1 fusion.30
  9.3 10.3 %all_gather.3 = bf16[1,512,768]{2,1,0:T(8,128)(2,1)S(1)} all-gather(bf16[1,128,768]{2,1,0:T(8,128)(2,1)S(1)} %fusion.30), channel_id=1, replica_groups=mesh['seq'=4,'batch'=8] {'seq'}, dimensions={1}, use_global_device_ids=true | all-gather | bytes 983040 | tf_op jit(solution)/shard_map/all_gather | solution.py:57
  19.7 0.0 all-to-all-done
  19.7 0.2 reshape.17
  19.9 0.2 copy.9
  20.1 0.4 convolution_bitcast_fusion.1
  20.5 0.4 convolution_bitcast_fusion.2
  20.8 0.3 convolution_bitcast_fusion
  21.2 0.1 fusion
  21.3 1.9 %copy.10 = f32[192,3,768]{0,2,1:T(8,128)} copy(f32[192,3,768]{2,0,1:T(8,128)S(1)} %fusion) | data formatting | bytes 3538944 | tf_op jit(solution)/shard_map/mul | solution.py:69
  23.3 0.0 copy-start
  23.3 6.5 %all-to-all-start.1 = ((f32[192,8,288]{0,2,1:T(8,128)}), f32[192,8,288]{0,2,1:T(8,128)S(1)}, u32[]{:S(2)}, u32[]{:S(2)}) async-start(f32[192,8,288]{0,2,1:T(8,128)} %bitcast.72), calls=%async_computation.1 | async-start | bytes 4718592 | tf_op jit(solution)/shard_map/all_to_all | solution.py:71
  29.7 0.0 copy-done
  29.8 2.0 %collective-permute-start.1 = (bf16[1,64,768]{2,1,0:T(8,128)(2,1)S(1)}, bf16[1,64,768]{2,1,0:T(8,128)(2,1)S(1)}, u32[]{:S(2)}, u32[]{:S(2)}) collective-permute-start(bf16[1,64,768]{2,1,0:T(8,128)(2,1)S(1)} %get-tuple-element.5), channel_id=1, source_target_pairs={{0,8},{8,16},{16,24},{1,9},{9,17},{17,25},{2,10},{10,18},{18,26},{... | collective-permute-start | bytes 294920 | tf_op jit(solution)/shard_map/ppermute | solution.py:18
  31.8 1.3 %collective-permute-start = (bf16[1,64,768]{2,1,0:T(8,128)(2,1)S(1)}, bf16[1,64,768]{2,1,0:T(8,128)(2,1)S(1)}, u32[]{:S(2)}, u32[]{:S(2)}) collective-permute-start(bf16[1,64,768]{2,1,0:T(8,128)(2,1)S(1)} %get-tuple-element.4), channel_id=1, source_target_pairs={{8,0},{16,8},{24,16},{9,1},{17,9},{25,17},{10,2},{18,10},{26,18},{... | collective-permute-start | bytes 294920 | tf_op jit(solution)/shard_map/ppermute | solution.py:19
  33.1 1.6 %fusion.5 = f32[128,768]{1,0:T(8,128)S(1)} fusion(bf16[768,2304]{1,0:T(8,128)(2,1)} %param.5, bf16[1,128,768]{2,1,0:T(8,128)(2,1)S(1)} %copy-done), kind=kOutput, calls=%fused_computation.10 | convolution fusion | flops 150994944 | bytes 1769472 | tf_op jit(solution)/shard_map/dot_general | solution.py:44
  34.7 0.0 collective-permute-done.1
  34.7 1.6 %fusion.3 = f32[128,768]{1,0:T(8,128)S(1)} fusion(bf16[768,2304]{1,0:T(8,128)(2,1)} %param.5, bf16[1,128,768]{2,1,0:T(8,128)(2,1)S(1)} %copy-done, bf16[1,64,768]{2,1,0:T(8,128)(2,1)S(1)} %collective-permute-done.1), kind=kOutput, calls=%fused_computation.8 | convolution fusion | flops 151388160 | bytes 1867776 | tf_op jit(solution)/shard_map/dot_general | solution.py:44
  36.3 0.0 collective-permute-done
  36.3 2.4 %fusion.11 = bf16[1,128,768]{2,1,0:T(8,128)(2,1)} fusion(f32[128,768]{1,0:T(8,128)S(1)} %fusion.3, f32[128,768]{1,0:T(8,128)S(1)} %fusion.5, bf16[768,2304]{1,0:T(8,128)(2,1)} %param.5, bf16[1,128,768]{2,1,0:T(8,128)(2,1)S(1)} %copy-done.1, bf16[1,64,768]{2,1,0:T(8,128)(2,1)S(1)} %collective-permute-done, bf16[1,128,768]{2,1,0:T(8,128)(2,1)S(1)} %copy-done), kind=kOutput, calls=%fused_computation.14 | convolution fusion | flops 152666112 | bytes 2654208 | tf_op jit(solution)/shard_map/dot_general | solution.py:44
  38.6 45.5 %all-to-all-done.1 = f32[192,8,288]{0,2,1:T(8,128)S(1)} async-done(((f32[192,8,288]{0,2,1:T(8,128)}), f32[192,8,288]{0,2,1:T(8,128)S(1)}, u32[]{:S(2)}, u32[]{:S(2)}) %all-to-all-start.1) | async-done | bytes 1769504 | tf_op jit(solution)/shard_map/all_to_all | solution.py:71
  84.1 0.2 reduce_sum.9
  84.3 0.9 %copy.11 = f32[192,288]{1,0:T(8,128)} copy(f32[192,288]{0,1:T(8,128)S(1)} %reduce_sum.9) | data formatting | bytes 442368
  (3 shorter events, 0.1 us)
Async XLA Ops:
  0.6 8.6 %copy-start.1 = (bf16[1,128,768]{2,1,0:T(8,128)(2,1)S(1)}, bf16[1,128,768]{2,1,0:T(8,128)(2,1)}, u32[]{:S(2)}) copy-start(bf16[1,128,768]{2,1,0:T(8,128)(2,1)} %param.3) | copy-start | bytes 589828
  5.0 14.7 %all-to-all-start = ((bf16[4,2,12288]{2,1,0:T(2,128)(2,1)}), bf16[4,2,12288]{2,1,0:T(2,128)(2,1)S(1)}, u32[]{:S(2)}, u32[]{:S(2)}) async-start(bf16[4,2,12288]{2,1,0:T(2,128)(2,1)} %reshape.16), calls=%async_computation | async-start | bytes 393216 | tf_op jit(solution)/shard_map/all_to_all | solution.py:54
  23.3 6.5 %copy-start = (bf16[1,128,768]{2,1,0:T(8,128)(2,1)S(1)}, bf16[1,128,768]{2,1,0:T(8,128)(2,1)}, u32[]{:S(2)}) copy-start(bf16[1,128,768]{2,1,0:T(8,128)(2,1)} %param.4) | copy-start | bytes 589828
  23.3 60.9 %all-to-all-start.1 = ((f32[192,8,288]{0,2,1:T(8,128)}), f32[192,8,288]{0,2,1:T(8,128)S(1)}, u32[]{:S(2)}, u32[]{:S(2)}) async-start(f32[192,8,288]{0,2,1:T(8,128)} %bitcast.72), calls=%async_computation.1 | async-start | bytes 4718592 | tf_op jit(solution)/shard_map/all_to_all | solution.py:71
  29.8 4.9 %collective-permute-start.1 = (bf16[1,64,768]{2,1,0:T(8,128)(2,1)S(1)}, bf16[1,64,768]{2,1,0:T(8,128)(2,1)S(1)}, u32[]{:S(2)}, u32[]{:S(2)}) collective-permute-start(bf16[1,64,768]{2,1,0:T(8,128)(2,1)S(1)} %get-tuple-element.5), channel_id=1, source_target_pairs={{0,8},{8,16},{16,24},{1,9},{9,17},{17,25},{2,10},{10,18},{18,26},{... | collective-permute-start | bytes 294920 | tf_op jit(solution)/shard_map/ppermute | solution.py:18
  31.8 4.5 %collective-permute-start = (bf16[1,64,768]{2,1,0:T(8,128)(2,1)S(1)}, bf16[1,64,768]{2,1,0:T(8,128)(2,1)S(1)}, u32[]{:S(2)}, u32[]{:S(2)}) collective-permute-start(bf16[1,64,768]{2,1,0:T(8,128)(2,1)S(1)} %get-tuple-element.4), channel_id=1, source_target_pairs={{8,0},{16,8},{24,16},{9,1},{17,9},{25,17},{10,2},{18,10},{26,18},{... | collective-permute-start | bytes 294920 | tf_op jit(solution)/shard_map/ppermute | solution.py:19
where the time goes:
time: 85.6 us; the launch traced here: 85.2 us
  waiting for transfers between devices  45.5 us (53%)
  starting transfers between devices  14 us (16%)
  blocking collectives  10.3 us (12%)
  matrix products  6.62 us (8%)
  local copies, waits for them, and re-layouts  5.77 us (7%)
  other arithmetic  2.18 us (3%)
    all_to_all x1, waiting for transfers between devices, body(): lax.all_to_all(pieces, 'batch', split_axis=1, concat_axis=1, tiled=True)  45.5 us
    all_gather x1, blocking collectives, body(): whole_act = lax.all_gather(act[None], 'seq', axis=1, tiled=True)[0]  10.3 us
    all_to_all x1, starting transfers between devices, body(): lax.all_to_all(pieces, 'batch', split_axis=1, concat_axis=1, tiled=True)  6.48 us
    dot_general x3, matrix products, body(): jnp.dot(window, weight[:, tap_index * in_width:(tap_index + 1) * in_width...  5.54 us
    all_to_all x1, starting transfers between devices, body(): lax.all_to_all(cotangent, 'seq', split_axis=2, concat_axis=1, tiled=True)[0]  4.24 us
    unnamed x11, local copies, waits for them, and re-layouts  3.66 us
    ppermute x1, starting transfers between devices, extended_2(): before = lax.ppermute(last, axis, up)  1.98 us
    mul x1, local copies, waits for them, and re-layouts, body(): jnp.transpose(taps_sum, (1, 0, 2)).reshape(own_rows, KW * in_width) * factor  1.95 us
  transfers between devices with their start and end apart: 4, of which 1 were waited for; matrix products, arithmetic and copies ran while one was open for 7% of the time, Pallas kernels for 0%

commit v1 on v0

--- a/solution.py
+++ b/solution.py
@@ -1,3 +1,4 @@
+import functools
 import math
 import jax
 import jax.numpy as jnp
@@ -6,6 +7,29 @@
 
 KW = 3
 TAP_SPACING = 64
+
+
+def _replace_stops_all(panel, row_axis):
+    tile_out, far_arr = (lax.axis_size(row_axis), lax.axis_index(row_axis))
+    k_now = list(panel.shape)
+    res = panel.shape[2] // tile_out
+    k_now[2] = res
+    block_next = k_now[1]
+    k_now[1] = block_next * tile_out
+    b_next = jnp.zeros(k_now, panel.dtype)
+    for j0 in range(tile_out):
+        t1 = lax.dynamic_slice_in_dim(panel, (far_arr ^ j0) * res, res, axis=2)
+        if j0:
+            t1 = lax.ppermute(
+                t1,
+                axis_name=row_axis,
+                perm=list(map(lambda hop_no: (hop_no, hop_no ^ j0), range(tile_out))),
+            )
+        b_next = lax.dynamic_update_slice_in_dim(b_next, t1, (far_arr ^ j0) * block_next, axis=1)
+    return b_next
+
+
+scan_the_table = functools.partial(_replace_stops_all, row_axis="seq")
 
 
 def extended_2(x, sides, width):
@@ -51,7 +75,7 @@
     batch_count = lax.axis_size("batch")
     counted = batch_count * inputs.shape[0] * length * seq_count
     factor = 1.0 / math.sqrt(float(counted))
-    owned = lax.all_to_all(cotangent, "seq", split_axis=2, concat_axis=1, tiled=True)[0]
+    owned = scan_the_table(cotangent)[0]
     own_rows = owned.shape[1]
     owned_padded = jnp.pad(owned, ((reach, reach), (0, 0)))
     whole_act = lax.all_gather(act[None], "seq", axis=1, tiled=True)[0]

time: 85.6 us -> 79.9 us (0.933)
  local copies, waits for them, and re-layouts: 5.77 us -> 4.11 us
  starting transfers between devices: 14 us -> 12.5 us
  blocking collectives: 10.3 us -> 8.83 us
  other arithmetic: 2.18 us -> 1.3 us
    all_to_all x1 -> x0, starting transfers between devices: 4.24 us -> none  [body(): lax.all_to_all(cotangent, 'seq', split_axis=2, concat_axis=1, tiled=True)[0]]
    ppermute x0 -> x3, starting transfers between devices: none -> 3.18 us  [_replace_stops_all(): lax.ppermute(t1, axis_name=row_axis, perm=list(map(lambda hop_no: (hop_no...]
    unnamed x11 -> x5, local copies, waits for them, and re-layouts: 3.66 us -> 0.88 us
    unnamed x1 -> x0, other arithmetic: 1.81 us -> none
    all_gather x1, blocking collectives: 10.3 us -> 8.83 us  [body(): whole_act = lax.all_gather(act[None], 'seq', axis=1, tiled=True)[0]]
    dynamic_slice x0 -> x1, local copies, waits for them, and re-layouts: none -> 1.15 us  [_replace_stops_all(): t1 = lax.dynamic_slice_in_dim(panel, (far_arr ^ j0) * res, res, axis=2)]
    convert_element_type x1, other arithmetic: 0.09 us -> 1.02 us  [body(): act = activation.astype(jnp.bfloat16)]
  transfers between devices with their start and end apart: 4 -> 6, of which waited for: 1 -> 1; matrix products, arithmetic and copies ran while one was open for 7% -> 8% of each run, Pallas kernels for 0% -> 0%
where the time goes in v1:
time: 79.9 us; the launch traced here: 79.5 us
  waiting for transfers between devices  45.3 us (57%)
  starting transfers between devices  12.5 us (16%)
  blocking collectives  8.83 us (11%)
  matrix products  6.58 us (8%)
  local copies, waits for them, and re-layouts  4.11 us (5%)
  other arithmetic  1.3 us (2%)
  between operations  0.85 us (1%)
    all_to_all x1, waiting for transfers between devices, body(): lax.all_to_all(pieces, 'batch', split_axis=1, concat_axis=1, tiled=True)  45.3 us
    all_gather x1, blocking collectives, body(): whole_act = lax.all_gather(act[None], 'seq', axis=1, tiled=True)[0]  8.83 us
    all_to_all x1, starting transfers between devices, body(): lax.all_to_all(pieces, 'batch', split_axis=1, concat_axis=1, tiled=True)  5.9 us
    dot_general x3, matrix products, body(): jnp.dot(window, weight[:, tap_index * in_width:(tap_index + 1) * in_width...  5.55 us
    ppermute x3, starting transfers between devices, _replace_stops_all(): lax.ppermute(t1, axis_name=row_axis, perm=list(map(lambda hop_no: (hop_no...  3.18 us
    ppermute x1, starting transfers between devices, extended_2(): before = lax.ppermute(last, axis, up)  1.98 us
    mul x1, local copies, waits for them, and re-layouts, body(): jnp.transpose(taps_sum, (1, 0, 2)).reshape(own_rows, KW * in_width) * factor  1.92 us
  transfers between devices with their start and end apart: 6, of which 1 were waited for; matrix products, arithmetic and copies ran while one was open for 8% of the time, Pallas kernels for 0%

profile of v1, /device:TPU:0, one launch (start us, length us, event | category | flops | bytes accessed | tf_op | source)
XLA Modules:
  0.0 79.5 jit_solution(9160871531086692010)
XLA Ops:
  0.6 0.0 copy-start
  0.7 1.2 %constant_dynamic-slice_fusion = (bf16[1,128,192]{2,1,0:T(8,128)(2,1)S(1)}, bf16[1,128,192]{2,1,0:T(8,128)(2,1)S(1)}, bf16[1,128,192]{2,1,0:T(8,128)(2,1)S(1)}) fusion(bf16[1,128,768]{2,1,0:T(8,128)(2,1)} %param.4, s32[]{:T(128)S(6)} %select_n.30, s32[]{:T(128)S(6)} %select_n.26, s32[]{:T(128)S(6)} %select_n.28), kind=kLoop, calls=%fused_computation.48 | loop fusion | bytes 294924 | tf_op jit(solution)/shard_map/dynamic_slice | solution.py:21
  1.8 0.5 collective-permute-start.2
  2.3 2.6 %collective-permute-start.3 = (bf16[1,128,192]{2,1,0:T(8,128)(2,1)S(1)}, bf16[1,128,192]{2,1,0:T(8,128)(2,1)S(1)}, u32[]{:S(2)}, u32[]{:S(2)}) collective-permute-start(bf16[1,128,192]{2,1,0:T(8,128)(2,1)S(1)} %get-tuple-element.6), channel_id=1, source_target_pairs={{0,16},{8,24},{16,0},{24,8},{1,17},{9,25},{17,1},{25,9},{2,18},{10... | collective-permute-start | bytes 147464 | tf_op jit(solution)/shard_map/ppermute | solution.py:23
  4.9 0.1 collective-permute-start.4
  5.0 1.0 %fusion.30 = bf16[1,128,768]{2,1,0:T(8,128)(2,1)S(1)} fusion(bf16[1,128,768]{2,1,0:T(8,128)(2,1)} %param.3), kind=kLoop, calls=%fused_computation.34 | loop fusion | flops 589824 | bytes 393216 | tf_op jit(solution)/shard_map/convert_element_type | solution.py:63
  6.0 8.8 %all_gather.3 = bf16[1,512,768]{2,1,0:T(8,128)(2,1)S(1)} all-gather(bf16[1,128,768]{2,1,0:T(8,128)(2,1)S(1)} %fusion.30), channel_id=1, replica_groups=mesh['seq'=4,'batch'=8] {'seq'}, dimensions={1}, use_global_device_ids=true | all-gather | bytes 983040 | tf_op jit(solution)/shard_map/all_gather | solution.py:81
  14.9 0.0 copy-done
  14.9 0.1 bitcast_dynamic-update-slice_fusion.3
  15.0 0.0 collective-permute-done.2
  15.0 0.0 collective-permute-done.3
  15.1 0.0 collective-permute-done.4
  15.1 0.3 convolution_bitcast_fusion
  15.4 0.3 convolution_bitcast_fusion.1
  15.8 0.3 convolution_bitcast_fusion.2
  16.1 0.1 fusion
  16.3 1.9 %copy.6 = f32[192,3,768]{0,2,1:T(8,128)} copy(f32[192,3,768]{2,0,1:T(8,128)S(1)} %fusion) | data formatting | bytes 3538944 | tf_op jit(solution)/shard_map/mul | solution.py:93
  18.2 5.9 %all-to-all-start = ((f32[192,8,288]{0,2,1:T(8,128)}), f32[192,8,288]{0,2,1:T(8,128)S(1)}, u32[]{:S(2)}, u32[]{:S(2)}) async-start(f32[192,8,288]{0,2,1:T(8,128)} %bitcast.66), calls=%async_computation | async-start | bytes 4718592 | tf_op jit(solution)/shard_map/all_to_all | solution.py:95
  24.1 2.0 %collective-permute-start.1 = (bf16[1,64,768]{2,1,0:T(8,128)(2,1)S(1)}, bf16[1,64,768]{2,1,0:T(8,128)(2,1)S(1)}, u32[]{:S(2)}, u32[]{:S(2)}) collective-permute-start(bf16[1,64,768]{2,1,0:T(8,128)(2,1)S(1)} %get-tuple-element.8), channel_id=1, source_target_pairs={{0,8},{8,16},{16,24},{1,9},{9,17},{17,25},{2,10},{10,18},{18,26},{... | collective-permute-start | bytes 294920 | tf_op jit(solution)/shard_map/ppermute | solution.py:42
  26.1 0.0 copy-start.1
  26.1 1.4 %collective-permute-start = (bf16[1,64,768]{2,1,0:T(8,128)(2,1)S(1)}, bf16[1,64,768]{2,1,0:T(8,128)(2,1)S(1)}, u32[]{:S(2)}, u32[]{:S(2)}) collective-permute-start(bf16[1,64,768]{2,1,0:T(8,128)(2,1)S(1)} %get-tuple-element.7), channel_id=1, source_target_pairs={{8,0},{16,8},{24,16},{9,1},{17,9},{25,17},{10,2},{18,10},{26,18},{... | collective-permute-start | bytes 294920 | tf_op jit(solution)/shard_map/ppermute | solution.py:43
  27.5 1.6 %fusion.5 = f32[128,768]{1,0:T(8,128)S(1)} fusion(bf16[768,2304]{1,0:T(8,128)(2,1)} %param.5, bf16[1,128,768]{2,1,0:T(8,128)(2,1)S(1)} %copy-done), kind=kOutput, calls=%fused_computation.10 | convolution fusion | flops 150994944 | bytes 1769472 | tf_op jit(solution)/shard_map/dot_general | solution.py:68
  29.1 0.0 collective-permute-done.1
  29.2 1.6 %fusion.3 = f32[128,768]{1,0:T(8,128)S(1)} fusion(bf16[768,2304]{1,0:T(8,128)(2,1)} %param.5, bf16[1,128,768]{2,1,0:T(8,128)(2,1)S(1)} %copy-done, bf16[1,64,768]{2,1,0:T(8,128)(2,1)S(1)} %collective-permute-done.1), kind=kOutput, calls=%fused_computation.8 | convolution fusion | flops 151388160 | bytes 1867776 | tf_op jit(solution)/shard_map/dot_general | solution.py:68
  30.8 0.0 collective-permute-done
  30.8 0.0 copy-done.1
  30.8 2.4 %fusion.11 = bf16[1,128,768]{2,1,0:T(8,128)(2,1)} fusion(f32[128,768]{1,0:T(8,128)S(1)} %fusion.3, f32[128,768]{1,0:T(8,128)S(1)} %fusion.5, bf16[768,2304]{1,0:T(8,128)(2,1)} %param.5, bf16[1,128,768]{2,1,0:T(8,128)(2,1)S(1)} %copy-done.1, bf16[1,64,768]{2,1,0:T(8,128)(2,1)S(1)} %collective-permute-done, bf16[1,128,768]{2,1,0:T(8,128)(2,1)S(1)} %copy-done), kind=kOutput, calls=%fused_computation.14 | convolution fusion | flops 152666112 | bytes 2654208 | tf_op jit(solution)/shard_map/dot_general | solution.py:68
  33.1 45.3 %all-to-all-done = f32[192,8,288]{0,2,1:T(8,128)S(1)} async-done(((f32[192,8,288]{0,2,1:T(8,128)}), f32[192,8,288]{0,2,1:T(8,128)S(1)}, u32[]{:S(2)}, u32[]{:S(2)}) %all-to-all-start) | async-done | bytes 1769504 | tf_op jit(solution)/shard_map/all_to_all | solution.py:95
  78.5 0.2 reduce_sum.9
  78.6 0.9 %copy.7 = f32[192,288]{1,0:T(8,128)} copy(f32[192,288]{0,1:T(8,128)S(1)} %reduce_sum.9) | data formatting | bytes 442368
  (5 shorter events, 0.1 us)
Async XLA Ops:
  0.6 14.3 %copy-start = (bf16[1,128,768]{2,1,0:T(8,128)(2,1)S(1)}, bf16[1,128,768]{2,1,0:T(8,128)(2,1)}, u32[]{:S(2)}) copy-start(bf16[1,128,768]{2,1,0:T(8,128)(2,1)} %param.4) | copy-start | bytes 589828
  1.8 13.2 %collective-permute-start.2 = (bf16[1,128,192]{2,1,0:T(8,128)(2,1)S(1)}, bf16[1,128,192]{2,1,0:T(8,128)(2,1)S(1)}, u32[]{:S(2)}, u32[]{:S(2)}) collective-permute-start(bf16[1,128,192]{2,1,0:T(8,128)(2,1)S(1)} %get-tuple-element.5), channel_id=1, source_target_pairs={{0,8},{8,0},{16,24},{24,16},{1,9},{9,1},{17,25},{25,17},{2,10},{10... | collective-permute-start | bytes 147464 | tf_op jit(solution)/shard_map/ppermute | solution.py:23
  2.3 12.7 %collective-permute-start.3 = (bf16[1,128,192]{2,1,0:T(8,128)(2,1)S(1)}, bf16[1,128,192]{2,1,0:T(8,128)(2,1)S(1)}, u32[]{:S(2)}, u32[]{:S(2)}) collective-permute-start(bf16[1,128,192]{2,1,0:T(8,128)(2,1)S(1)} %get-tuple-element.6), channel_id=1, source_target_pairs={{0,16},{8,24},{16,0},{24,8},{1,17},{9,25},{17,1},{25,9},{2,18},{10... | collective-permute-start | bytes 147464 | tf_op jit(solution)/shard_map/ppermute | solution.py:23
  4.9 10.1 %collective-permute-start.4 = (bf16[1,128,192]{2,1,0:T(8,128)(2,1)S(1)}, bf16[1,128,192]{2,1,0:T(8,128)(2,1)S(1)}, u32[]{:S(2)}, u32[]{:S(2)}) collective-permute-start(bf16[1,128,192]{2,1,0:T(8,128)(2,1)S(1)} %get-tuple-element.4), channel_id=1, source_target_pairs={{0,24},{8,16},{16,8},{24,0},{1,25},{9,17},{17,9},{25,1},{2,26},{10... | collective-permute-start | bytes 147464 | tf_op jit(solution)/shard_map/ppermute | solution.py:23
  18.2 60.3 %all-to-all-start = ((f32[192,8,288]{0,2,1:T(8,128)}), f32[192,8,288]{0,2,1:T(8,128)S(1)}, u32[]{:S(2)}, u32[]{:S(2)}) async-start(f32[192,8,288]{0,2,1:T(8,128)} %bitcast.66), calls=%async_computation | async-start | bytes 4718592 | tf_op jit(solution)/shard_map/all_to_all | solution.py:95
  24.1 5.0 %collective-permute-start.1 = (bf16[1,64,768]{2,1,0:T(8,128)(2,1)S(1)}, bf16[1,64,768]{2,1,0:T(8,128)(2,1)S(1)}, u32[]{:S(2)}, u32[]{:S(2)}) collective-permute-start(bf16[1,64,768]{2,1,0:T(8,128)(2,1)S(1)} %get-tuple-element.8), channel_id=1, source_target_pairs={{0,8},{8,16},{16,24},{1,9},{9,17},{17,25},{2,10},{10,18},{18,26},{... | collective-permute-start | bytes 294920 | tf_op jit(solution)/shard_map/ppermute | solution.py:42
  26.1 4.7 %copy-start.1 = (bf16[1,128,768]{2,1,0:T(8,128)(2,1)S(1)}, bf16[1,128,768]{2,1,0:T(8,128)(2,1)}, u32[]{:S(2)}) copy-start(bf16[1,128,768]{2,1,0:T(8,128)(2,1)} %param.3) | copy-start | bytes 589828
  26.1 4.7 %collective-permute-start = (bf16[1,64,768]{2,1,0:T(8,128)(2,1)S(1)}, bf16[1,64,768]{2,1,0:T(8,128)(2,1)S(1)}, u32[]{:S(2)}, u32[]{:S(2)}) collective-permute-start(bf16[1,64,768]{2,1,0:T(8,128)(2,1)S(1)} %get-tuple-element.7), channel_id=1, source_target_pairs={{8,0},{16,8},{24,16},{9,1},{17,9},{25,17},{10,2},{18,10},{26,18},{... | collective-permute-start | bytes 294920 | tf_op jit(solution)/shard_map/ppermute | solution.py:43
